TPU v7x, 32 devices: a whole 2x2x4 slice. The times are simulated.
32 devices in a mesh: grp: 2 (over y), outer: 4 (over x, core), inner: 4 (over z).
Axes of the slice: x: 2, y: 2, z: 4, core: 2. Of those that a mesh axis runs over, the one named last changes fastest.
Arguments:
- query: bfloat16 [4096, 1024], P(('grp', 'outer', 'inner')), parts along dimension 0, may hold values from -6 to 6
- key: bfloat16 [4096, 1024], P(('grp', 'outer', 'inner')), parts along dimension 0, may hold values from -6 to 6
- value: bfloat16 [4096, 1024], P(('grp', 'outer', 'inner')), parts along dimension 0, may hold values from -6 to 6
- grad_out: bfloat16 [4096, 1024], P(('grp', 'outer', 'inner')), parts along dimension 0, may hold values from -6 to 6
Outputs:
- normed_out: bfloat16 [4096, 1024], P(('grp', 'outer', 'inner')), parts along dimension 0
- grad_query: bfloat16 [4096, 1024], P(('grp', 'outer', 'inner')), parts along dimension 0
- grad_key: bfloat16 [4096, 1024], P(('grp', 'outer', 'inner')), parts along dimension 0
- grad_value: bfloat16 [4096, 1024], P(('grp', 'outer', 'inner')), parts along dimension 0
There are 2 independent parts, one for each index of `grp`. A program takes and returns all parts, laid end to end along the dimension named above; each array names one. Nothing has to cross between parts.
All inputs are finite; a program needn't handle non-finite values.
Results may differ from a plain program's by a relative error of at most 0.0059.
Values sent between devices are 32-bit elements; how exact they have to be, the bound alone decides.
No kernel may reach another device: no remote copies, remote signals or barrier semaphores. Data moves between devices by JAX's collectives and lax.ppermute only.
A program may use at most 64 MiB of HBM per device.

v0:
```python
import jax
import jax.numpy as jnp
from jax import lax
from jax.sharding import PartitionSpec as P

HEADS = 8
HEAD = 128


def carried_in(value, axis, join, neutral, backward):
    count, mine = (lax.axis_size(axis), lax.axis_index(axis))
    pieces = lax.all_gather(value, axis)
    if backward:
        pieces = pieces[::-1]
        mine = count - 1 - mine
    running = jnp.full_like(value, 0) + jnp.asarray(neutral, value.dtype)

    def lap(position, running):
        longer = join(running, pieces[position])
        return jnp.where(position < mine, longer, running)

    return lax.fori_loop(0, count - 1, lap, running)


def add_terms(earlier, later):
    return earlier + later


def forward_prefix(state):
    empty_state = jnp.zeros_like(state)
    inner_prior = carried_in(state, "inner", add_terms, empty_state, False)
    row_total = lax.psum(state, "inner")
    return carried_in(row_total, "outer", add_terms, empty_state, False) + inner_prior


def backward_suffix(state):
    empty_state = jnp.zeros_like(state)
    inner_later = carried_in(state, "inner", add_terms, empty_state, True)
    row_total = lax.psum(state, "inner")
    return carried_in(row_total, "outer", add_terms, empty_state, True) + inner_later


def per_device(query, key, value, grad_out):
    rows_dev = query.shape[0]
    scaling = HEAD ** (-0.5)
    queries = query.reshape(rows_dev, HEADS, HEAD)
    key_rows = key.reshape(rows_dev, HEADS, HEAD)
    value_rows = value.reshape(rows_dev, HEADS, HEAD)
    line = lax.broadcasted_iota(jnp.int32, (rows_dev, rows_dev), 0)
    column = lax.broadcasted_iota(jnp.int32, (rows_dev, rows_dev), 1)
    causal = (line >= column)[None]
    state = jnp.einsum("thi,thj->hij", key_rows, value_rows, preferred_element_type=jnp.float32)
    prior = forward_prefix(state)
    prior_half = prior.astype(jnp.bfloat16)
    scores = (
        jnp.einsum("thi,shi->hts", queries, key_rows, preferred_element_type=jnp.float32) * scaling
    )
    score_half = jnp.where(causal, scores, 0.0).astype(jnp.bfloat16)
    attended = jnp.einsum(
        "hts,shj->thj", score_half, value_rows, preferred_element_type=jnp.float32
    )
    attended = attended + scaling * jnp.einsum(
        "thi,hij->thj", queries, prior_half, preferred_element_type=jnp.float32
    )
    flat = attended.reshape(rows_dev, HEADS * HEAD)
    inverse = lax.rsqrt(jnp.mean(flat * flat, axis=-1, keepdims=True) + 1e-05)
    normed = flat * inverse
    grads_flat = grad_out.astype(jnp.float32)
    grad_pre = inverse * (
        grads_flat - normed * jnp.mean(grads_flat * normed, axis=-1, keepdims=True)
    )
    grad_half = grad_pre.astype(jnp.bfloat16).reshape(rows_dev, HEADS, HEAD)
    dscores = jnp.einsum("thj,shj->hts", grad_half, value_rows, preferred_element_type=jnp.float32)
    dscore_half = jnp.where(causal, dscores, 0.0).astype(jnp.bfloat16)
    grad_q = jnp.einsum("hts,shi->thi", dscore_half, key_rows, preferred_element_type=jnp.float32)
    grad_q = scaling * (
        grad_q
        + jnp.einsum("thj,hij->thi", grad_half, prior_half, preferred_element_type=jnp.float32)
    )
    grad_state = jnp.einsum("thi,thj->hij", queries, grad_half, preferred_element_type=jnp.float32)
    later = backward_suffix(grad_state)
    later_half = later.astype(jnp.bfloat16)
    grad_k = jnp.einsum("hts,thi->shi", dscore_half, queries, preferred_element_type=jnp.float32)
    grad_k = scaling * (
        grad_k
        + jnp.einsum("shj,hij->shi", value_rows, later_half, preferred_element_type=jnp.float32)
    )
    grad_v = jnp.einsum("hts,thj->shj", score_half, grad_half, preferred_element_type=jnp.float32)
    grad_v = grad_v + scaling * jnp.einsum(
        "shi,hij->shj", key_rows, later_half, preferred_element_type=jnp.float32
    )
    width = HEADS * HEAD
    return (
        normed.astype(jnp.bfloat16),
        grad_q.reshape(rows_dev, width).astype(jnp.bfloat16),
        grad_k.reshape(rows_dev, width).astype(jnp.bfloat16),
        grad_v.reshape(rows_dev, width).astype(jnp.bfloat16),
    )


def solution(mesh):
    placed = (
        P(("grp", "outer", "inner"), None),
        P(("grp", "outer", "inner"), None),
        P(("grp", "outer", "inner"), None),
        P(("grp", "outer", "inner"), None),
    )
    return jax.shard_map(
        per_device,
        mesh=mesh,
        in_specs=placed,
        out_specs=(
            P(("grp", "outer", "inner"), None),
            P(("grp", "outer", "inner"), None),
            P(("grp", "outer", "inner"), None),
            P(("grp", "outer", "inner"), None),
        ),
        check_vma=False,
    )
```

profile of v0, /device:TPU:0, one launch (start us, length us, event | category | flops | bytes accessed | tf_op | source)
XLA Modules:
  0.0 253.9 jit_solution(7140993363098596042)
XLA Ops:
  7.2 1.1 copy.62
  8.3 0.2 copy.35
  8.6 1.0 fusion.19
  9.6 48.5 %all-gather.11.cloned.1.call-done = f32[32,128,128]{2,1,0:T(8,128)} async-done(((f32[8,128,128]{2,1,0:T(8,128)}), f32[32,128,128]{2,1,0:T(8,128)}) %all-gather.11.cloned.1.call-update) | async-done | bytes 2097168 | tf_op jit(solution)/shard_map/all_gather | solution.py:12
  58.1 0.7 all-reduce.3.cloned.1.call-update
  58.9 39.7 %all-reduce.3.cloned.1.call-done = f32[1,8,128,128]{3,2,1,0:T(8,128)} async-done(((f32[1,8,128,128]{3,2,1,0:T(8,128)}), f32[1,8,128,128]{3,2,1,0:T(8,128)}) %all-reduce.3.cloned.1.call-update) | async-done | bytes 524304 | tf_op jit(solution)/shard_map/psum | solution.py:32
  98.7 0.3 fusion.8
  99.0 3.8 %while.57 = (s32[]{:T(128)}, f32[8,128,128]{2,1,0:T(8,128)S(1)}, s32[]{:T(128)}, f32[4,8,128,128]{3,2,1,0:T(8,128)}, s32[]{:T(128)}, /*index=5*/s32[]{:T(128)}) while((s32[]{:T(128)}, f32[8,128,128]{2,1,0:T(8,128)S(1)}, s32[]{:T(128)}, f32[4,8,128,128]{3,2,1,0:T(8,128)}, s32[]{:T(128)}, /*index=5*/s32[]{:T(128)}) %tuple.146), condition=%wide.region_4.5_spmd.clone, body=%wide.region_3.4_spmd.clone.sunk | while | flops 393220 | bytes 1572957 | solution.py:22
  99.1 1.2 add_select_fusion.9
  100.3 1.2 add_select_fusion.9
  101.6 1.2 add_select_fusion.9
  102.8 19.8 %all-gather.7.cloned.1.call-done = f32[4,8,128,128]{3,2,1,0:T(8,128)} async-done(((f32[1,8,128,128]{3,2,1,0:T(8,128)}), f32[4,8,128,128]{3,2,1,0:T(8,128)}) %all-gather.7.cloned.1.call-update) | async-done | bytes 2097168 | tf_op jit(solution)/shard_map/all_gather | solution.py:12
  122.6 3.7 %while.56 = (s32[]{:T(128)}, f32[8,128,128]{2,1,0:T(8,128)S(1)}, s32[]{:T(128)}, f32[4,8,128,128]{3,2,1,0:T(8,128)}, s32[]{:T(128)}, /*index=5*/s32[]{:T(128)}) while((s32[]{:T(128)}, f32[8,128,128]{2,1,0:T(8,128)S(1)}, s32[]{:T(128)}, f32[4,8,128,128]{3,2,1,0:T(8,128)}, s32[]{:T(128)}, /*index=5*/s32[]{:T(128)}) %tuple.122), condition=%wide.region_2.3_spmd.clone, body=%wide.region_1.2_spmd.clone.sunk | while | flops 393220 | bytes 1572957 | solution.py:22
  122.6 1.2 add_select_fusion.8
  123.9 1.2 add_select_fusion.8
  125.1 1.2 add_select_fusion.8
  126.4 0.3 fusion.6
  126.8 0.4 multiply_reduce_fusion
  127.1 0.2 copy.39
  127.4 0.2 fusion.13
  127.6 0.9 fusion.15
  128.6 0.2 fusion.24
  128.9 1.0 copy.48
  129.9 0.5 all-reduce.5.cloned.1.call-update
  130.5 0.5 all-gather.13.cloned.1.call-update
  131.1 40.3 %all-reduce.5.cloned.1.call-done = f32[1,8,128,128]{2,3,1,0:T(8,128)} async-done(((f32[1,8,128,128]{2,3,1,0:T(8,128)}), f32[1,8,128,128]{2,3,1,0:T(8,128)}) %all-reduce.5.cloned.1.call-update) | async-done | bytes 524304 | tf_op jit(solution)/shard_map/psum | solution.py:39
  171.4 2.0 copy.47
  173.5 0.3 fusion.12
  173.8 0.2 convolution_bitcast_fusion.2
  174.0 0.3 fusion.11
  174.3 0.9 copy.53
  175.2 1.0 fusion.38
  176.2 1.1 convolution_bitcast_fusion
  177.3 41.0 %all-gather.13.cloned.1.call-done = f32[32,128,128]{2,1,0:T(8,128)} async-done(((f32[8,128,128]{2,1,0:T(8,128)}), f32[32,128,128]{2,1,0:T(8,128)}) %all-gather.13.cloned.1.call-update) | async-done | bytes 2097168 | tf_op jit(solution)/shard_map/all_gather | solution.py:12
  218.3 1.7 rev.7
  220.0 0.6 while.59
  220.1 0.2 add_select_fusion.11
  220.3 0.2 add_select_fusion.11
  220.5 0.2 add_select_fusion.11
  220.6 20.5 %all-gather.9.cloned.1.call-done = f32[4,8,128,128]{3,2,1,0:T(8,128)} async-done(((f32[1,8,128,128]{3,2,1,0:T(8,128)}), f32[4,8,128,128]{3,2,1,0:T(8,128)}) %all-gather.9.cloned.1.call-update) | async-done | bytes 2097168 | tf_op jit(solution)/shard_map/all_gather | solution.py:12
  241.1 1.7 rev.6
  242.9 0.6 while.58
  242.9 0.2 add_select_fusion.10
  243.1 0.2 add_select_fusion.10
  243.5 1.5 fusion.9
  245.0 0.9 copy.55
  245.9 0.3 fusion.10
  246.2 0.9 copy.54
  (32 shorter events, 0.8 us)
Async XLA Ops:
  7.2 1.4 copy-start
  7.2 91.5 %copy-start.4 = (bf16[128,1024]{1,0:T(8,128)(2,1)S(1)}, bf16[128,1024]{1,0:T(8,128)(2,1)}, u32[]{:S(2)}) copy-start(bf16[128,1024]{1,0:T(8,128)(2,1)} %param.13) | copy-start | bytes 786436
  7.2 91.5 %copy-start.2 = (bf16[128,1024]{1,0:T(8,128)(2,1)S(1)}, bf16[128,1024]{1,0:T(8,128)(2,1)}, u32[]{:S(2)}) copy-start(bf16[128,1024]{1,0:T(8,128)(2,1)} %param.12) | copy-start | bytes 786436
  7.2 50.9 %all-gather.11.cloned.1.call-start = ((), (), s32[]{:S(2)}) async-start(), calls=%async_computation.4 | async-start | bytes 2621440 | tf_op jit(solution)/shard_map/all_gather | solution.py:12
  58.1 40.5 %all-reduce.3.cloned.1.call-start = ((), (), s32[]{:S(2)}) async-start(), calls=%async_computation | async-start | bytes 1048576 | tf_op jit(solution)/shard_map/psum | solution.py:32
  58.9 63.7 %all-gather.7.cloned.1.call-start = ((), (), s32[]{:S(2)}) async-start(), calls=%async_computation.1 | async-start | bytes 2621440 | tf_op jit(solution)/shard_map/all_gather | solution.py:12
  126.4 1.0 copy-start.5
  128.9 1.0 copy-start.1
  129.9 41.5 %all-reduce.5.cloned.1.call-start = ((), (), s32[]{:S(2)}) async-start(), calls=%async_computation.2 | async-start | bytes 1048576 | tf_op jit(solution)/shard_map/psum | solution.py:39
  130.5 87.9 %all-gather.13.cloned.1.call-start = ((), (), s32[]{:S(2)}) async-start(), calls=%async_computation.5 | async-start | bytes 2621440 | tf_op jit(solution)/shard_map/all_gather | solution.py:12
  131.0 110.1 %all-gather.9.cloned.1.call-start = ((), (), s32[]{:S(2)}) async-start(), calls=%async_computation.3 | async-start | bytes 2621440 | tf_op jit(solution)/shard_map/all_gather | solution.py:12
  243.5 2.4 copy-start.3
Sparse Core Ops, SparseCore 0:
  9.7 48.3 all-gather.10
  61.3 37.3 all-reduce.2
  100.2 22.3 all-gather.6
  132.7 38.6 all-reduce.4
  172.8 45.4 all-gather.12
  219.7 21.3 all-gather.8
where the time goes:
time: 254 us
  waiting for transfers between devices  212 us (83%)
  between operations  14.4 us (6%)
  local copies, waits for them, and re-layouts  10.8 us (4%)
  other arithmetic  9.62 us (4%)
  matrix products  6.99 us (3%)
    all_gather x4, waiting for transfers between devices, carried_in(): pieces = lax.all_gather(value, axis)  130 us
    psum x1, waiting for transfers between devices, backward_suffix(): row_total = lax.psum(state, 'inner')  40.3 us
    psum x1, waiting for transfers between devices, forward_prefix(): row_total = lax.psum(state, 'inner')  39.7 us
    select_n x12, other arithmetic, lap(): return jnp.where(position < mine, longer, running)  8.37 us
  transfers between devices with their start and end apart: 6, of which 6 were waited for; matrix products, arithmetic and copies ran while one was open for 5% of the time, Pallas kernels for 0%

commit v1 on v0

--- a/solution.py
+++ b/solution.py
@@ -29,7 +29,7 @@
 def forward_prefix(state):
     empty_state = jnp.zeros_like(state)
     inner_prior = carried_in(state, "inner", add_terms, empty_state, False)
-    row_total = lax.psum(state, "inner")
+    row_total = jnp.sum(lax.all_gather(state, "inner"), axis=0)
     return carried_in(row_total, "outer", add_terms, empty_state, False) + inner_prior
 
 

time: 254 us -> 214 us (0.84)
  waiting for transfers between devices: 212 us -> 169 us
  other arithmetic: 9.62 us -> 12.2 us
    all_gather x4 -> x3, waiting for transfers between devices: 130 us -> 78.9 us  [carried_in(): pieces = lax.all_gather(value, axis)]
    all_gather x0 -> x1, waiting for transfers between devices: none -> 48.5 us  [forward_prefix(): row_total = jnp.sum(lax.all_gather(state, 'inner'), axis=0)]
    psum x1 -> x0, waiting for transfers between devices: 39.7 us -> none  [forward_prefix(): row_total = lax.psum(state, 'inner')]
    reduce_sum x0 -> x1, other arithmetic: none -> 2.55 us  [forward_prefix(): row_total = jnp.sum(lax.all_gather(state, 'inner'), axis=0)]
  transfers between devices with their start and end apart: 6 -> 5, of which waited for: 6 -> 5; matrix products, arithmetic and copies ran while one was open for 5% -> 6% of each run, Pallas kernels for 0% -> 0%
where the time goes in v1:
time: 214 us; the launch traced here: 213 us
  waiting for transfers between devices  169 us (79%)
  between operations  14 us (7%)
  other arithmetic  12.2 us (6%)
  local copies, waits for them, and re-layouts  10.7 us (5%)
  matrix products  6.98 us (3%)
    all_gather x3, waiting for transfers between devices, carried_in(): pieces = lax.all_gather(value, axis)  78.9 us
    all_gather x1, waiting for transfers between devices, forward_prefix(): row_total = jnp.sum(lax.all_gather(state, 'inner'), axis=0)  48.5 us
    psum x1, waiting for transfers between devices, backward_suffix(): row_total = lax.psum(state, 'inner')  40.5 us
    select_n x12, other arithmetic, lap(): return jnp.where(position < mine, longer, running)  8.37 us
  transfers between devices with their start and end apart: 5, of which 5 were waited for; matrix products, arithmetic and copies ran while one was open for 6% of the time, Pallas kernels for 0%

profile of v1, /device:TPU:0, one launch (start us, length us, event | category | flops | bytes accessed | tf_op | source)
XLA Modules:
  0.0 213.4 jit_solution(11320547761382715132)
XLA Ops:
  7.2 1.0 copy.62
  8.3 0.2 copy.35
  8.5 1.0 fusion.19
  9.6 48.5 %all-gather.10.cloned.1.call-done = f32[32,128,128]{2,1,0:T(8,128)} async-done(((f32[8,128,128]{2,1,0:T(8,128)}), f32[32,128,128]{2,1,0:T(8,128)}) %all-gather.10.cloned.1.call-update) | async-done | bytes 2097168 | tf_op jit(solution)/shard_map/all_gather | solution.py:32
  58.1 2.6 %reduce_sum.27 = f32[8,128,128]{2,1,0:T(8,128)} reduce(f32[4,8,128,128]{3,2,1,0:T(8,128)} %bitcast.129, f32[]{:T(128)} %constant.104.clone.1), dimensions={0}, to_apply=%region_0.1 | reduce | flops 393216 | bytes 2621444 | tf_op jit(solution)/shard_map/reduce_sum | solution.py:32
  60.7 0.3 fusion.8
  61.1 3.8 %while.57 = (s32[]{:T(128)}, f32[8,128,128]{2,1,0:T(8,128)S(1)}, s32[]{:T(128)}, f32[4,8,128,128]{3,2,1,0:T(8,128)}, s32[]{:T(128)}, /*index=5*/s32[]{:T(128)}) while((s32[]{:T(128)}, f32[8,128,128]{2,1,0:T(8,128)S(1)}, s32[]{:T(128)}, f32[4,8,128,128]{3,2,1,0:T(8,128)}, s32[]{:T(128)}, /*index=5*/s32[]{:T(128)}) %tuple.144), condition=%wide.region_4.5_spmd.clone, body=%wide.region_3.4_spmd.clone.sunk | while | flops 393220 | bytes 1572957 | solution.py:22
  61.1 1.2 add_select_fusion.9
  62.3 1.2 add_select_fusion.9
  63.6 1.2 add_select_fusion.9
  64.8 17.4 %all-gather.12.cloned.1.call-done = f32[32,128,128]{2,1,0:T(8,128)} async-done(((f32[8,128,128]{2,1,0:T(8,128)}), f32[32,128,128]{2,1,0:T(8,128)}) %all-gather.12.cloned.1.call-update) | async-done | bytes 2097168 | tf_op jit(solution)/shard_map/all_gather | solution.py:12
  82.2 3.7 %while.56 = (s32[]{:T(128)}, f32[8,128,128]{2,1,0:T(8,128)S(1)}, s32[]{:T(128)}, f32[4,8,128,128]{3,2,1,0:T(8,128)}, s32[]{:T(128)}, /*index=5*/s32[]{:T(128)}) while((s32[]{:T(128)}, f32[8,128,128]{2,1,0:T(8,128)S(1)}, s32[]{:T(128)}, f32[4,8,128,128]{3,2,1,0:T(8,128)}, s32[]{:T(128)}, /*index=5*/s32[]{:T(128)}) %tuple.145), condition=%wide.region_2.3_spmd.clone, body=%wide.region_1.2_spmd.clone.sunk | while | flops 393220 | bytes 1572957 | solution.py:22
  82.2 1.2 add_select_fusion.8
  83.4 1.2 add_select_fusion.8
  84.7 1.2 add_select_fusion.8
  86.0 0.3 fusion.6
  86.3 0.4 multiply_reduce_fusion
  86.7 0.2 copy.39
  86.9 0.2 fusion.13
  87.2 0.9 fusion.15
  88.2 0.2 fusion.24
  88.5 1.0 copy.48
  89.5 0.7 all-reduce.2.cloned.1.call-update
  90.2 0.5 all-gather.14.cloned.1.call-update
  90.8 40.5 %all-reduce.2.cloned.1.call-done = f32[1,8,128,128]{2,3,1,0:T(8,128)} async-done(((f32[1,8,128,128]{2,3,1,0:T(8,128)}), f32[1,8,128,128]{2,3,1,0:T(8,128)}) %all-reduce.2.cloned.1.call-update) | async-done | bytes 524304 | tf_op jit(solution)/shard_map/psum | solution.py:39
  131.3 2.0 copy.47
  133.4 0.3 fusion.12
  133.7 0.2 convolution_bitcast_fusion.2
  133.9 0.3 fusion.11
  134.2 0.9 copy.53
  135.1 1.0 fusion.38
  136.1 1.1 convolution_bitcast_fusion
  137.2 41.0 %all-gather.14.cloned.1.call-done = f32[32,128,128]{2,1,0:T(8,128)} async-done(((f32[8,128,128]{2,1,0:T(8,128)}), f32[32,128,128]{2,1,0:T(8,128)}) %all-gather.14.cloned.1.call-update) | async-done | bytes 2097168 | tf_op jit(solution)/shard_map/all_gather | solution.py:12
  178.2 1.7 rev.7
  179.9 0.6 while.59
  180.0 0.2 add_select_fusion.11
  180.1 0.2 add_select_fusion.11
  180.3 0.2 add_select_fusion.11
  180.5 20.5 %all-gather.8.cloned.1.call-done = f32[4,8,128,128]{3,2,1,0:T(8,128)} async-done(((f32[1,8,128,128]{3,2,1,0:T(8,128)}), f32[4,8,128,128]{3,2,1,0:T(8,128)}) %all-gather.8.cloned.1.call-update) | async-done | bytes 2097168 | tf_op jit(solution)/shard_map/all_gather | solution.py:12
  201.0 1.7 rev.6
  202.7 0.6 while.58
  202.8 0.2 add_select_fusion.10
  203.0 0.2 add_select_fusion.10
  203.2 0.2 add_select_fusion.10
  203.4 1.5 fusion.9
  204.9 0.9 copy.55
  205.8 0.3 fusion.10
  206.1 0.9 copy.54
  (30 shorter events, 0.6 us)
Async XLA Ops:
  7.2 1.3 copy-start
  7.2 50.9 %all-gather.10.cloned.1.call-start = ((), (), s32[]{:S(2)}) async-start(), calls=%async_computation.2 | async-start | bytes 2621440 | tf_op jit(solution)/shard_map/all_gather | solution.py:32
  9.5 51.2 %copy-start.2 = (bf16[128,1024]{1,0:T(8,128)(2,1)S(1)}, bf16[128,1024]{1,0:T(8,128)(2,1)}, u32[]{:S(2)}) copy-start(bf16[128,1024]{1,0:T(8,128)(2,1)} %param.12) | copy-start | bytes 786436
  9.5 51.2 %copy-start.4 = (bf16[128,1024]{1,0:T(8,128)(2,1)S(1)}, bf16[128,1024]{1,0:T(8,128)(2,1)}, u32[]{:S(2)}) copy-start(bf16[128,1024]{1,0:T(8,128)(2,1)} %param.13) | copy-start | bytes 786436
  9.6 72.6 %all-gather.12.cloned.1.call-start = ((), (), s32[]{:S(2)}) async-start(), calls=%async_computation.3 | async-start | bytes 2621440 | tf_op jit(solution)/shard_map/all_gather | solution.py:12
  86.0 1.0 copy-start.5
  88.5 1.0 copy-start.1
  89.5 41.8 %all-reduce.2.cloned.1.call-start = ((), (), s32[]{:S(2)}) async-start(), calls=%async_computation | async-start | bytes 1048576 | tf_op jit(solution)/shard_map/psum | solution.py:39
  90.2 88.0 %all-gather.14.cloned.1.call-start = ((), (), s32[]{:S(2)}) async-start(), calls=%async_computation.4 | async-start | bytes 2621440 | tf_op jit(solution)/shard_map/all_gather | solution.py:12
  90.8 110.2 %all-gather.8.cloned.1.call-start = ((), (), s32[]{:S(2)}) async-start(), calls=%async_computation.1 | async-start | bytes 2621440 | tf_op jit(solution)/shard_map/all_gather | solution.py:12
  203.3 2.4 %copy-start.3 = (f32[128,8,128]{0,2,1:T(8,128)S(1)}, f32[128,8,128]{0,2,1:T(8,128)}, u32[]{:S(2)}) copy-start(f32[128,8,128]{0,2,1:T(8,128)} %convolution_bitcast_fusion) | copy-start | bytes 1572868
Sparse Core Ops, SparseCore 0:
  9.7 48.3 all-gather.9
  60.8 21.3 all-gather.11
  92.6 38.6 all-reduce.1
  132.7 45.4 all-gather.13
  179.6 21.3 all-gather.7
